TPU v7x, 32 devices: a whole 2x2x4 slice. The times are simulated.
32 devices in a mesh: groups: 2 (over y), gz: 4 (over z), sec: 2 (over x), ch: 2 (over core).
Axes of the slice: x: 2, y: 2, z: 4, core: 2. Of those that a mesh axis runs over, the one named last changes fastest.
Arguments:
- coarse: bfloat16 [64, 32, 4, 256], P('ch', ('groups', 'gz', 'sec')), parts along dimension 1, may hold values from -6 to 6
- saved_pre: bfloat16 [32, 64, 8, 512], P('ch', ('groups', 'gz', 'sec')), parts along dimension 1, may hold values from -6 to 6
- out_grad: bfloat16 [32, 64, 8, 512], P('ch', ('groups', 'gz', 'sec')), parts along dimension 1, may hold values from -6 to 6
- up_weight: bfloat16 [27, 32, 64], replicated, may hold values from -0.21875 to 0.21875
- refine_weight: bfloat16 [27, 32, 32], replicated, may hold values from -0.21875 to 0.21875
Outputs:
- grad_coarse: bfloat16 [64, 32, 4, 256], P('ch', ('groups', 'gz', 'sec')), parts along dimension 1
- grad_up: float32 [54, 32, 64], P('groups', 'ch'), parts along dimension 0
- grad_refine: float32 [54, 32, 32], P('groups', None, 'ch'), parts along dimension 0
There are 2 independent parts, one for each index of `groups`. A program takes and returns all parts, laid end to end along the dimension named above; an argument that names none is the same for every part. Nothing has to cross between parts.
All inputs are finite; a program needn't handle non-finite values.
Results may differ from a plain program's by a relative error of at most 0.0049.
Values may be sent and summed in bfloat16 or wider, within the bound.
No kernel may reach another device: no remote copies, remote signals or barrier semaphores. Data moves between devices by JAX's collectives and lax.ppermute only.
A program may use at most 128 MiB of HBM per device.

v0:
```python
import jax
import jax.numpy as jnp
from jax import lax
from jax.sharding import PartitionSpec as P

leak_slope = 0.2
SPATIAL = ("NCDHW", "OIDHW", "NCDHW")


def padded(block, sides, width):
    for axis, dim in sides:
        count = lax.axis_size(axis)
        forward = [(i, i + 1) for i in range(count - 1)]
        forward.append((count - 1, 0))
        backward = [(target, source) for source, target in forward]
        low = lax.ppermute(
            lax.slice_in_dim(block, block.shape[dim] - width, None, axis=dim), axis, forward
        )
        high = lax.ppermute(lax.slice_in_dim(block, 0, width, axis=dim), axis, backward)
        block = jnp.concatenate([low, block, high], axis=dim)
    return block


def passed_along(block, axis, distance):
    devices = range(lax.axis_size(axis))
    route = [((i - distance) % len(devices), i) for i in devices]
    return lax.ppermute(block, axis, route)


def wrap_y(block, low, high):
    size = block.shape[3]
    parts = [block[:, :, :, size - low :], block, block[:, :, :, :high]]
    return jnp.concatenate([p for p in parts if p.shape[3]], axis=3)


def conv(lhs, rhs, strides, dilation):
    return lax.conv_general_dilated(
        lhs,
        rhs,
        window_strides=strides,
        padding="VALID",
        rhs_dilation=dilation,
        dimension_numbers=SPATIAL,
        preferred_element_type=jnp.float32,
    )


def filter_grad(lhs, cotangent, strides, dilation):
    return lax.conv_general_dilated(
        lhs,
        cotangent,
        window_strides=strides,
        padding="VALID",
        rhs_dilation=dilation,
        dimension_numbers=("CNDHW", "IODHW", "CNDHW"),
        preferred_element_type=jnp.float32,
    )


def local(coarse, saved_pre, out_grad, up_weight, refine_weight):
    part_ch = saved_pre.shape[0]
    planes_z = saved_pre.shape[1]
    planes_x = saved_pre.shape[2]
    cells_y = saved_pre.shape[3]
    channel_start = lax.axis_index("ch") * part_ch
    pre_act = saved_pre.astype(jnp.float32)
    slopes = jnp.where(pre_act > 0, 1.0, leak_slope).astype(jnp.float32)
    hidden = (pre_act * slopes).astype(jnp.bfloat16)
    rimmed_local = padded(out_grad, ((("gz", "sec"), 1),), 2)
    every_channel = lax.all_gather(rimmed_local, "ch", axis=0, tiled=True)
    rimmed = jnp.pad(every_channel, ((0, 0), (0, 0), (2, 2), (0, 0)))
    rimmed = wrap_y(rimmed, 2, 2)[None]
    refine_cols = lax.dynamic_slice_in_dim(refine_weight, channel_start, part_ch, 2)
    refine_k = refine_cols.reshape(3, 3, 3, refine_cols.shape[1], part_ch)[::-1, ::-1, ::-1]
    refine_k = jnp.transpose(refine_k, (4, 3, 0, 1, 2))
    grad_hidden = conv(rimmed, refine_k, (1, 1, 1), (2, 2, 2))[0]
    refine_grad_k = filter_grad(rimmed, hidden[None], (2, 2, 2), (1, 1, 1))
    refine_terms = jnp.transpose(refine_grad_k[:, :, ::-1, ::-1, ::-1], (2, 3, 4, 1, 0))
    refine_terms = refine_terms.reshape(27, refine_cols.shape[1], part_ch)
    grad_pre = (grad_hidden * slopes).astype(jnp.bfloat16)
    below_z = passed_along(grad_pre[:, planes_z - 1 :, :, :], ("gz", "sec"), 1)
    raised_z = jnp.concatenate([below_z, grad_pre], axis=1)
    extended = jnp.pad(raised_z, ((0, 0), (0, 0), (1, 0), (0, 0)))
    extended = wrap_y(extended, 1, 0)[None]
    all_coarse = lax.all_gather(coarse, "ch", axis=0, tiled=True)
    up_rows = lax.dynamic_slice_in_dim(up_weight, channel_start, part_ch, 1)
    up_k = jnp.transpose(up_rows.reshape(3, 3, 3, part_ch, up_rows.shape[2]), (4, 3, 0, 1, 2))
    running = conv(extended, up_k, (2, 2, 2), (1, 1, 1))
    up_grad_k = filter_grad(extended, all_coarse[None], (1, 1, 1), (2, 2, 2))
    up_terms = jnp.transpose(up_grad_k, (2, 3, 4, 1, 0)).reshape(27, part_ch, up_rows.shape[2])
    coarse_summed = lax.psum_scatter(running[0], "ch", scatter_dimension=0, tiled=True)
    grad_coarse = coarse_summed.astype(jnp.bfloat16)
    flat = jnp.concatenate([up_terms.reshape(-1), refine_terms.reshape(-1)])
    flat = lax.psum(flat, ("gz", "sec"))
    up_summed = flat[: up_terms.size].reshape(up_terms.shape)
    refine_summed = flat[up_terms.size :].reshape(refine_terms.shape)
    fine_total = planes_z * lax.axis_size("gz") * lax.axis_size("sec") * planes_x * cells_y
    coarse_total = fine_total // 8
    grad_up = up_summed * float(coarse_total) ** (-0.5)
    grad_refine = refine_summed * float(fine_total) ** (-0.5)
    return (grad_coarse, grad_up, grad_refine)


def solution(mesh):
    placed = (
        P("ch", ("groups", "gz", "sec"), None, None),
        P("ch", ("groups", "gz", "sec"), None, None),
        P("ch", ("groups", "gz", "sec"), None, None),
        P(),
        P(),
    )
    return jax.shard_map(
        local,
        mesh=mesh,
        in_specs=placed,
        out_specs=(
            P("ch", ("groups", "gz", "sec"), None, None),
            P("groups", "ch", None),
            P("groups", None, "ch"),
        ),
        check_vma=False,
    )
```

profile of v0, /device:TPU:0, one launch (start us, length us, event | category | flops | bytes accessed | tf_op | source)
XLA Modules:
  0.0 495.4 jit_solution(4544733990261625754)
XLA Ops:
  7.2 1.2 fusion.36
  8.4 6.0 %collective-permute-start.1 = (bf16[16,2,8,512]{3,2,1,0:T(8,128)(2,1)S(1)}, bf16[16,2,8,512]{3,2,1,0:T(8,128)(2,1)S(1)}, u32[]{:S(2)}, u32[]{:S(2)}) collective-permute-start(bf16[16,2,8,512]{3,2,1,0:T(8,128)(2,1)S(1)} %get-tuple-element.21), channel_id=1, source_target_pairs={{2,0},{4,2},{6,4},{8,6},{10,8},{12,10},{14,12},{0,14},{3,1},{5,3},... | collective-permute-start | bytes 786440 | tf_op jit(solution)/shard_map/ppermute | solution.py:19
  14.4 5.6 %collective-permute-done.1 = bf16[16,2,8,512]{3,2,1,0:T(8,128)(2,1)S(1)} collective-permute-done((bf16[16,2,8,512]{3,2,1,0:T(8,128)(2,1)S(1)}, bf16[16,2,8,512]{3,2,1,0:T(8,128)(2,1)S(1)}, u32[]{:S(2)}, u32[]{:S(2)}) %collective-permute-start.1) | collective-permute-done | bytes 262176 | tf_op jit(solution)/shard_map/ppermute | solution.py:19
  20.0 4.9 collective-permute-done
  24.9 2.1 pad_maximum_fusion.1
  27.1 1.2 dynamic-slice
  29.0 0.9 copy.63
  29.9 2.0 all_gather.7
  31.9 2.0 copy.65
  33.9 0.7 constant_dynamic-slice_fusion
  34.7 3.3 all-gather.2.cloned.1.call-done
  38.0 2.5 copy.53
  40.5 0.3 pad_slice_fusion.1
  40.8 0.4 pad.8
  41.2 4.0 fusion.23
  45.2 2.3 pad.10
  47.5 10.9 %reshape.30 = bf16[32,8,12,1,8,65]{5,4,1,2,0,3:T(8,128)(2,1)} reshape(bf16[32,8,12,1,520]{4,1,2,0,3:T(8,128)(2,1)} %pad.10) | data formatting | bytes 6389760 | tf_op jit(solution)/shard_map/conv_general_dilated | solution.py:37
  58.4 17.4 %copy.55 = bf16[32,8,12,1,8,65]{0,4,5,2,1,3:T(8,128)(2,1)} copy(bf16[32,8,12,1,8,65]{5,4,1,2,0,3:T(8,128)(2,1)} %reshape.30) | data formatting | bytes 6389760 | tf_op jit(solution)/shard_map/conv_general_dilated | solution.py:37
  75.8 1.4 slice.44
  77.2 26.3 %broadcast_select_fusion = f32[4,8,8,65,16]{4,2,3,1,0:T(8,128)} fusion(pred[8,65]{0,1:T(8,128)(4,1)S(1)} %copy-done.8, bf16[3,3,3,32,16]{4,3,2,1,0:T(8,128)(2,1)S(1)} %bitcast.62, bf16[32,8,12,1,7,4]{0,4,5,2,1,3:T(8,128)(2,1)S(1)} %slice.44, bf16[32,8,12,1,8,65]{0,4,5,2,1,3:T(8,128)(2,1)} %copy.55), kind=kOutput, calls=%fused_computation.14 | convolution fusion | flops 470503424 | bytes 4460040 | tf_op jit(solution)/shard_map/conv_general_dilated | solution.py:37
  103.5 5.6 %copy.57 = f32[4,8,8,65,16]{3,2,4,1,0:T(8,128)S(1)} copy(f32[4,8,8,65,16]{4,2,3,1,0:T(8,128)} %broadcast_select_fusion) | data formatting | bytes 2129920 | tf_op jit(solution)/shard_map/conv_general_dilated | solution.py:37
  109.1 1.8 reshape.34
  110.9 1.7 fusion.29
  112.6 0.8 copy-done.2
  113.5 0.7 slice.46
  114.1 1.7 collective-permute-start.2
  115.8 43.9 %copy.66 = bf16[1,32,8,12,516]{1,0,4,3,2:T(2,128)(2,1)} copy(bf16[1,32,8,12,516]{4,2,3,1,0:T(8,128)(2,1)} %get-tuple-element.12) | data formatting | bytes 6340608 | tf_op jit(solution)/shard_map/broadcast_in_dim | solution.py:72
  159.7 14.3 %copy.67 = bf16[1,16,4,8,512]{1,0,4,3,2:T(2,128)(2,1)} copy(bf16[1,16,4,8,512]{4,1,3,2,0:T(8,128)(2,1)S(1)} %get-tuple-element.18) | data formatting | bytes 1048576 | tf_op jit(solution)/shard_map/broadcast_in_dim | solution.py:77
  174.0 172.7 %fusion.38 = f32[16,32,3,3,3]{1,0,4,3,2:T(8,128)S(1)} fusion(bf16[1,32,8,12,516]{1,0,4,3,2:T(2,128)(2,1)} %copy.66, bf16[1,16,4,8,512]{1,0,4,3,2:T(2,128)(2,1)} %copy.67), kind=kOutput, calls=%fused_computation.52 | convolution fusion | flops 452984832 | bytes 3749888 | tf_op jit(solution)/shard_map/conv_general_dilated | solution.py:49
  347.0 0.8 reshape_reshape.7
  347.8 1.0 fusion.26
  348.9 0.5 fusion.28
  349.5 1.5 reshape.37
  351.0 5.3 %copy.60 = bf16[16,5,9,1,8,66]{0,4,5,2,1,3:T(8,128)(2,1)} copy(bf16[16,5,9,1,8,66]{5,4,0,2,1,3:T(8,128)(2,1)S(1)} %reshape.37) | data formatting | bytes 1520640 | tf_op jit(solution)/shard_map/conv_general_dilated | solution.py:37
  356.4 1.0 slice.48
  357.3 8.2 %fusion.19 = f32[2,4,8,33,64]{4,2,3,1,0:T(8,128)S(1)} fusion(bf16[3,3,3,16,64]{4,3,2,1,0:T(8,128)(2,1)} %bitcast.63, bf16[16,5,9,1,7,2]{0,4,5,2,1,3:T(8,128)(2,1)S(1)} %slice.48, bf16[16,5,9,1,8,66]{0,4,5,2,1,3:T(8,128)(2,1)} %copy.60, pred[8,33]{0,1:T(8,128)(4,1)S(1)} %copy-done.9), kind=kOutput, calls=%fused_computation.22 | convolution fusion | flops 119270400 | bytes 1376712 | tf_op jit(solution)/shard_map/conv_general_dilated | solution.py:37
  365.5 0.3 copy.61
  365.9 0.4 copy.62
  366.3 21.1 %copy.64 = bf16[1,16,5,9,513]{1,0,4,3,2:T(2,128)(2,1)} copy(bf16[1,16,5,9,513]{4,1,3,2,0:T(8,128)(2,1)S(1)} %get-tuple-element.16) | data formatting | bytes 1477440 | tf_op jit(solution)/shard_map/broadcast_in_dim | solution.py:84
  387.5 26.9 %fusion.37 = f32[3,3,3,16,64]{4,3,2,1,0:T(8,128)S(1)} fusion(bf16[1,16,5,9,513]{1,0,4,3,2:T(2,128)(2,1)} %copy.64, bf16[1,64,2,4,256]{1,0,4,3,2:T(2,128)(2,1)S(1)} %copy-done.4), kind=kOutput, calls=%fused_computation.51 | convolution fusion | flops 113246208 | bytes 1111456 | tf_op jit(solution)/shard_map/transpose | solution.py:90
  414.5 0.7 pad_maximum_fusion.3
  415.2 4.8 all-reduce.7
  420.1 0.7 dynamic-slice_convert_fusion
  420.8 64.0 %all-reduce.6.cloned.1.call-done = f32[41472]{0:T(1024)} async-done(((f32[41472]{0:T(1024)}), f32[41472]{0:T(1024)}) %all-reduce.6.cloned.1.call-update) | async-done | bytes 165904 | tf_op jit(solution)/shard_map/psum | solution.py:94
  484.7 0.9 slice_multiply_fusion
  485.6 0.8 mul.32
  486.4 0.8 slice_multiply_fusion.1
  487.4 0.9 copy.69
  (33 shorter events, 1.0 us)
Async XLA Ops:
  7.2 26.7 %copy-start = (bf16[27,32,64]{2,1,0:T(8,128)(2,1)S(1)}, bf16[27,32,64]{2,1,0:T(8,128)(2,1)}, u32[]{:S(2)}) copy-start(bf16[27,32,64]{2,1,0:T(8,128)(2,1)} %param.8) | copy-start | bytes 331780
  7.2 27.4 %copy-start.7 = (bf16[27,32,32]{2,1,0:T(8,128)(2,1)S(1)}, bf16[27,32,32]{2,1,0:T(8,128)(2,1)}, u32[]{:S(2)}) copy-start(bf16[27,32,32]{2,1,0:T(8,128)(2,1)} %param.9) | copy-start | bytes 165892
  7.2 30.8 %all-gather.2.cloned.1.call-start = ((), (), s32[]{:S(2)}) async-start(), calls=%async_computation | async-start | bytes 3145728 | tf_op jit(solution)/shard_map/all_gather | solution.py:70
  8.4 11.6 %collective-permute-start.1 = (bf16[16,2,8,512]{3,2,1,0:T(8,128)(2,1)S(1)}, bf16[16,2,8,512]{3,2,1,0:T(8,128)(2,1)S(1)}, u32[]{:S(2)}, u32[]{:S(2)}) collective-permute-start(bf16[16,2,8,512]{3,2,1,0:T(8,128)(2,1)S(1)} %get-tuple-element.21), channel_id=1, source_target_pairs={{2,0},{4,2},{6,4},{8,6},{10,8},{12,10},{14,12},{0,14},{3,1},{5,3},... | collective-permute-start | bytes 786440 | tf_op jit(solution)/shard_map/ppermute | solution.py:19
  14.4 10.5 %collective-permute-start = (bf16[16,2,8,512]{3,2,1,0:T(8,128)(2,1)S(1)}, bf16[16,2,8,512]{3,2,1,0:T(8,128)(2,1)S(1)}, u32[]{:S(2)}, u32[]{:S(2)}) collective-permute-start(bf16[16,2,8,512]{3,2,1,0:T(8,128)(2,1)S(1)} %get-tuple-element.20), channel_id=1, source_target_pairs={{0,2},{2,4},{4,6},{6,8},{8,10},{10,12},{12,14},{14,0},{1,3},{3,5},... | collective-permute-start | bytes 786440 | tf_op jit(solution)/shard_map/ppermute | solution.py:16
  27.1 457.7 %all-reduce.6.cloned.1.call-start = ((), (), s32[]{:S(2)}) async-start(), calls=%async_computation.1 | async-start | bytes 335872 | tf_op jit(solution)/shard_map/psum | solution.py:94
  58.4 18.8 %copy-start.8 = (pred[8,65]{0,1:T(8,128)(4,1)S(1)}, pred[8,65]{0,1:T(8,128)(4,1)}, u32[]{:S(2)}) copy-start(pred[8,65]{0,1:T(8,128)(4,1)} %constant.38) | copy-start | bytes 1564
  103.5 7.4 %copy-start.5 = (bf16[16,4,8,512]{3,2,1,0:T(8,128)(2,1)S(1)}, bf16[16,4,8,512]{3,2,1,0:T(8,128)(2,1)}, u32[]{:S(2)}) copy-start(bf16[16,4,8,512]{3,2,1,0:T(8,128)(2,1)} %param.6) | copy-start | bytes 1572868
  112.6 0.8 copy-start.2
  114.1 233.7 %collective-permute-start.2 = (bf16[16,1,8,512]{3,0,2,1:T(8,128)(2,1)}, bf16[16,1,8,512]{3,0,2,1:T(8,128)(2,1)}, u32[]{:S(2)}, u32[]{:S(2)}) collective-permute-start(bf16[16,1,8,512]{3,0,2,1:T(8,128)(2,1)} %slice.46), channel_id=1, source_target_pairs={{14,0},{0,2},{2,4},{4,6},{6,8},{8,10},{10,12},{12,14},{15,1},{1,3}... | collective-permute-start | bytes 393224 | tf_op jit(solution)/shard_map/ppermute | solution.py:27
  174.0 173.8 %copy-start.3 = (bf16[16,4,8,512]{3,0,2,1:T(8,128)(2,1)S(1)}, bf16[16,4,8,512]{3,0,2,1:T(8,128)(2,1)}, u32[]{:S(2)}) copy-start(bf16[16,4,8,512]{3,0,2,1:T(8,128)(2,1)} %copy-done.2) | copy-start | bytes 1572868
  349.4 7.9 %copy-start.9 = (pred[8,33]{0,1:T(8,128)(4,1)S(1)}, pred[8,33]{0,1:T(8,128)(4,1)}, u32[]{:S(2)}) copy-start(pred[8,33]{0,1:T(8,128)(4,1)} %constant.37) | copy-start | bytes 796
  366.3 21.1 %copy-start.4 = (bf16[1,64,2,4,256]{1,0,4,3,2:T(2,128)(2,1)S(1)}, bf16[1,64,2,4,256]{1,0,4,3,2:T(2,128)(2,1)}, u32[]{:S(2)}) copy-start(bf16[1,64,2,4,256]{1,0,4,3,2:T(2,128)(2,1)} %copy.65) | copy-start | bytes 786436
  387.5 27.1 %copy-start.6 = (f32[13824]{0:T(1024)S(1)}, f32[13824]{0:T(1024)}, u32[]{:S(2)}) copy-start(f32[13824]{0:T(1024)} %reshape_reshape.7) | copy-start | bytes 165892
  387.5 100.8 %copy-start.1 = (bf16[27,32,64]{2,1,0:T(8,128)(2,1)S(1)}, bf16[27,32,64]{2,1,0:T(8,128)(2,1)}, u32[]{:S(2)}) copy-start(bf16[27,32,64]{2,1,0:T(8,128)(2,1)} %param.8) | copy-start | bytes 331780
Sparse Core Ops, SparseCore 0:
  27.2 10.7 all-gather.1
  415.3 69.3 all-reduce.5
where the time goes:
time: 504 us; the launch traced here: 495 us
  matrix products  234 us (46%)
  local copies, waits for them, and re-layouts  142 us (28%)
  waiting for transfers between devices  77.7 us (15%)
  between operations  15.2 us (3%)
  other arithmetic  11.8 us (2%)
  starting transfers between devices  7.84 us (2%)
  blocking collectives  6.82 us (1%)
    conv_general_dilated x1, matrix products, filter_grad(): lax.conv_general_dilated(lhs, cotangent, window_strides=strides, padding=...  173 us
    psum x1, waiting for transfers between devices, local(): flat = lax.psum(flat, ('gz', 'sec'))  64 us
    broadcast_in_dim x2, local copies, waits for them, and re-layouts, local(): rimmed = wrap_y(rimmed, 2, 2)[None]  46.2 us
    conv_general_dilated x9, local copies, waits for them, and re-layouts, conv(): lax.conv_general_dilated(lhs, rhs, window_strides=strides, padding='VALID...  45.2 us
    conv_general_dilated x2, matrix products, conv(): lax.conv_general_dilated(lhs, rhs, window_strides=strides, padding='VALID...  34.5 us
    transpose x1, matrix products, local(): jnp.transpose(up_grad_k, (2, 3, 4, 1, 0))  26.9 us
    broadcast_in_dim x2, local copies, waits for them, and re-layouts, local(): extended = wrap_y(extended, 1, 0)[None]  21.2 us
    broadcast_in_dim x1, local copies, waits for them, and re-layouts, local(): refine_grad_k = filter_grad(rimmed, hidden[None], (2, 2, 2), (1, 1, 1))  14.3 us
  transfers between devices with their start and end apart: 5, of which 4 were waited for; matrix products, arithmetic and copies ran while one was open for 48% of the time, Pallas kernels for 0%

commit v1 on v0

--- a/solution.py
+++ b/solution.py
@@ -5,6 +5,12 @@
 
 leak_slope = 0.2
 SPATIAL = ("NCDHW", "OIDHW", "NCDHW")
+
+
+def gather_and_add(value, name):
+    parts = lax.all_gather(value, name, axis=0, tiled=False)
+    summed = parts.sum(axis=0)
+    return summed
 
 
 def padded(block, sides, width):
@@ -91,7 +97,7 @@
     coarse_summed = lax.psum_scatter(running[0], "ch", scatter_dimension=0, tiled=True)
     grad_coarse = coarse_summed.astype(jnp.bfloat16)
     flat = jnp.concatenate([up_terms.reshape(-1), refine_terms.reshape(-1)])
-    flat = lax.psum(flat, ("gz", "sec"))
+    flat = gather_and_add(flat, ("gz", "sec"))
     up_summed = flat[: up_terms.size].reshape(up_terms.shape)
     refine_summed = flat[up_terms.size :].reshape(refine_terms.shape)
     fine_total = planes_z * lax.axis_size("gz") * lax.axis_size("sec") * planes_x * cells_y

time: 504 us -> 460 us (0.913)
  waiting for transfers between devices: 77.7 us -> 34.9 us
    psum x1 -> x0, waiting for transfers between devices: 64 us -> none  [local(): flat = lax.psum(flat, ('gz', 'sec'))]
    all_gather x0 -> x1, waiting for transfers between devices: none -> 18.6 us  [gather_and_add(): parts = lax.all_gather(value, name, axis=0, tiled=False)]
  transfers between devices with their start and end apart: 5 -> 5, of which waited for: 4 -> 4; matrix products, arithmetic and copies ran while one was open for 48% -> 56% of each run, Pallas kernels for 0% -> 0%
where the time goes in v1:
time: 460 us; the launch traced here: 451 us
  matrix products  234 us (51%)
  local copies, waits for them, and re-layouts  141 us (31%)
  waiting for transfers between devices  34.9 us (8%)
  between operations  15.2 us (3%)
  other arithmetic  11.7 us (3%)
  starting transfers between devices  7.84 us (2%)
  blocking collectives  6.82 us (1%)
    conv_general_dilated x1, matrix products, filter_grad(): lax.conv_general_dilated(lhs, cotangent, window_strides=strides, padding=...  173 us
    broadcast_in_dim x2, local copies, waits for them, and re-layouts, local(): rimmed = wrap_y(rimmed, 2, 2)[None]  46.2 us
    conv_general_dilated x9, local copies, waits for them, and re-layouts, conv(): lax.conv_general_dilated(lhs, rhs, window_strides=strides, padding='VALID...  45.2 us
    conv_general_dilated x2, matrix products, conv(): lax.conv_general_dilated(lhs, rhs, window_strides=strides, padding='VALID...  34.5 us
    transpose x1, matrix products, local(): jnp.transpose(up_grad_k, (2, 3, 4, 1, 0))  26.9 us
    broadcast_in_dim x2, local copies, waits for them, and re-layouts, local(): extended = wrap_y(extended, 1, 0)[None]  21.2 us
    all_gather x1, waiting for transfers between devices, gather_and_add(): parts = lax.all_gather(value, name, axis=0, tiled=False)  18.6 us
    broadcast_in_dim x1, local copies, waits for them, and re-layouts, local(): refine_grad_k = filter_grad(rimmed, hidden[None], (2, 2, 2), (1, 1, 1))  14.3 us
  transfers between devices with their start and end apart: 5, of which 4 were waited for; matrix products, arithmetic and copies ran while one was open for 56% of the time, Pallas kernels for 0%

profile of v1, /device:TPU:0, one launch (start us, length us, event | category | flops | bytes accessed | tf_op | source)
XLA Modules:
  0.0 451.5 jit_solution(1947083839620703508)
XLA Ops:
  7.2 1.2 fusion.36
  8.4 6.0 %collective-permute-start.1 = (bf16[16,2,8,512]{3,2,1,0:T(8,128)(2,1)S(1)}, bf16[16,2,8,512]{3,2,1,0:T(8,128)(2,1)S(1)}, u32[]{:S(2)}, u32[]{:S(2)}) collective-permute-start(bf16[16,2,8,512]{3,2,1,0:T(8,128)(2,1)S(1)} %get-tuple-element.21), channel_id=1, source_target_pairs={{2,0},{4,2},{6,4},{8,6},{10,8},{12,10},{14,12},{0,14},{3,1},{5,3},... | collective-permute-start | bytes 786440 | tf_op jit(solution)/shard_map/ppermute | solution.py:25
  14.4 5.6 %collective-permute-done.1 = bf16[16,2,8,512]{3,2,1,0:T(8,128)(2,1)S(1)} collective-permute-done((bf16[16,2,8,512]{3,2,1,0:T(8,128)(2,1)S(1)}, bf16[16,2,8,512]{3,2,1,0:T(8,128)(2,1)S(1)}, u32[]{:S(2)}, u32[]{:S(2)}) %collective-permute-start.1) | collective-permute-done | bytes 262176 | tf_op jit(solution)/shard_map/ppermute | solution.py:25
  20.0 4.9 %collective-permute-done = bf16[16,2,8,512]{3,2,1,0:T(8,128)(2,1)S(1)} collective-permute-done((bf16[16,2,8,512]{3,2,1,0:T(8,128)(2,1)S(1)}, bf16[16,2,8,512]{3,2,1,0:T(8,128)(2,1)S(1)}, u32[]{:S(2)}, u32[]{:S(2)}) %collective-permute-start) | collective-permute-done | bytes 262176 | tf_op jit(solution)/shard_map/ppermute | solution.py:22
  24.9 2.1 pad_maximum_fusion.1
  27.1 0.9 copy.63
  28.0 2.0 all_gather.13
  30.0 2.0 copy.65
  32.1 5.8 %all-gather.5.cloned.1.call-done = bf16[32,8,8,512]{3,2,1,0:T(8,128)(2,1)} async-done(((bf16[16,8,8,512]{3,2,1,0:T(8,128)(2,1)}), bf16[32,8,8,512]{3,2,1,0:T(8,128)(2,1)}) %all-gather.5.cloned.1.call-update) | async-done | bytes 2097168 | tf_op jit(solution)/shard_map/all_gather | solution.py:76
  37.9 2.5 copy.53
  40.4 0.3 pad_slice_fusion.1
  40.8 0.4 pad.8
  41.1 4.0 fusion.23
  45.2 2.3 pad.10
  47.4 10.9 %reshape.30 = bf16[32,8,12,1,8,65]{5,4,1,2,0,3:T(8,128)(2,1)} reshape(bf16[32,8,12,1,520]{4,1,2,0,3:T(8,128)(2,1)} %pad.10) | data formatting | bytes 6389760 | tf_op jit(solution)/shard_map/conv_general_dilated | solution.py:43
  58.3 17.4 %copy.55 = bf16[32,8,12,1,8,65]{0,4,5,2,1,3:T(8,128)(2,1)} copy(bf16[32,8,12,1,8,65]{5,4,1,2,0,3:T(8,128)(2,1)} %reshape.30) | data formatting | bytes 6389760 | tf_op jit(solution)/shard_map/conv_general_dilated | solution.py:43
  75.7 1.4 slice.44
  77.1 26.3 %broadcast_select_fusion = f32[4,8,8,65,16]{4,2,3,1,0:T(8,128)} fusion(pred[8,65]{0,1:T(8,128)(4,1)S(1)} %copy-done.7, bf16[3,3,3,32,16]{4,3,2,1,0:T(8,128)(2,1)S(1)} %bitcast.62, bf16[32,8,12,1,7,4]{0,4,5,2,1,3:T(8,128)(2,1)S(1)} %slice.44, bf16[32,8,12,1,8,65]{0,4,5,2,1,3:T(8,128)(2,1)} %copy.55), kind=kOutput, calls=%fused_computation.14 | convolution fusion | flops 470503424 | bytes 4460040 | tf_op jit(solution)/shard_map/conv_general_dilated | solution.py:43
  103.4 5.6 %copy.57 = f32[4,8,8,65,16]{3,2,4,1,0:T(8,128)S(1)} copy(f32[4,8,8,65,16]{4,2,3,1,0:T(8,128)} %broadcast_select_fusion) | data formatting | bytes 2129920 | tf_op jit(solution)/shard_map/conv_general_dilated | solution.py:43
  109.1 1.8 reshape.34
  110.9 1.7 fusion.29
  112.6 0.8 copy-done.1
  113.4 0.7 slice.46
  114.1 1.7 collective-permute-start.2
  115.8 43.9 %copy.66 = bf16[1,32,8,12,516]{1,0,4,3,2:T(2,128)(2,1)} copy(bf16[1,32,8,12,516]{4,2,3,1,0:T(8,128)(2,1)} %get-tuple-element.12) | data formatting | bytes 6340608 | tf_op jit(solution)/shard_map/broadcast_in_dim | solution.py:78
  159.7 14.3 %copy.67 = bf16[1,16,4,8,512]{1,0,4,3,2:T(2,128)(2,1)} copy(bf16[1,16,4,8,512]{4,1,3,2,0:T(8,128)(2,1)S(1)} %get-tuple-element.18) | data formatting | bytes 1048576 | tf_op jit(solution)/shard_map/broadcast_in_dim | solution.py:83
  174.0 172.8 %fusion.38 = f32[16,32,3,3,3]{1,0,4,3,2:T(8,128)S(1)} fusion(bf16[1,32,8,12,516]{1,0,4,3,2:T(2,128)(2,1)} %copy.66, bf16[1,16,4,8,512]{1,0,4,3,2:T(2,128)(2,1)} %copy.67), kind=kOutput, calls=%fused_computation.52 | convolution fusion | flops 452984832 | bytes 3749888 | tf_op jit(solution)/shard_map/conv_general_dilated | solution.py:55
  346.9 0.2 copy.68
  347.1 0.2 reshape_reshape.7
  347.3 1.0 fusion.26
  348.4 0.5 fusion.28
  348.9 21.1 %copy.64 = bf16[1,16,5,9,513]{1,0,4,3,2:T(2,128)(2,1)} copy(bf16[1,16,5,9,513]{4,1,3,2,0:T(8,128)(2,1)S(1)} %get-tuple-element.16) | data formatting | bytes 1477440 | tf_op jit(solution)/shard_map/broadcast_in_dim | solution.py:90
  370.0 26.9 %fusion.37 = f32[3,3,3,16,64]{4,3,2,1,0:T(8,128)S(1)} fusion(bf16[1,16,5,9,513]{1,0,4,3,2:T(2,128)(2,1)} %copy.64, bf16[1,64,2,4,256]{1,0,4,3,2:T(2,128)(2,1)S(1)} %copy-done.3), kind=kOutput, calls=%fused_computation.51 | convolution fusion | flops 113246208 | bytes 1111456 | tf_op jit(solution)/shard_map/transpose | solution.py:96
  397.1 0.8 reshape.53
  397.9 0.6 dynamic-slice
  399.3 1.5 reshape.37
  400.8 5.3 %copy.60 = bf16[16,5,9,1,8,66]{0,4,5,2,1,3:T(8,128)(2,1)} copy(bf16[16,5,9,1,8,66]{5,4,0,2,1,3:T(8,128)(2,1)S(1)} %reshape.37) | data formatting | bytes 1520640 | tf_op jit(solution)/shard_map/conv_general_dilated | solution.py:43
  406.1 1.0 slice.48
  407.2 8.2 %fusion.19 = f32[2,4,8,33,64]{4,2,3,1,0:T(8,128)S(1)} fusion(bf16[3,3,3,16,64]{4,3,2,1,0:T(8,128)(2,1)S(1)} %bitcast.63, bf16[16,5,9,1,7,2]{0,4,5,2,1,3:T(8,128)(2,1)S(1)} %slice.48, bf16[16,5,9,1,8,66]{0,4,5,2,1,3:T(8,128)(2,1)} %copy.60, pred[8,33]{0,1:T(8,128)(4,1)S(1)} %copy-done.8), kind=kOutput, calls=%fused_computation.22 | convolution fusion | flops 119270400 | bytes 1376712 | tf_op jit(solution)/shard_map/conv_general_dilated | solution.py:43
  415.3 0.3 copy.61
  415.7 0.4 copy.62
  416.1 4.8 %all-reduce.4 = bf16[64,2,4,256]{3,2,1,0:T(4,128)(2,1)S(1)} all-reduce(f32[64,2,4,256]{3,2,1,0:T(4,128)S(1)} %copy.62), channel_id=3, replica_groups=mesh['groups'=2,'gz'=4,'sec'=2,'ch'=2] {'ch'}, use_global_device_ids=true, to_apply=%region_0.1.clone | all-reduce | flops 131072 | bytes 786432
  420.9 0.7 dynamic-slice_convert_fusion
  421.6 18.6 %all-gather.7.cloned.1.call-done = f32[8,1,41472]{2,1,0:T(1,128)} async-done(((f32[1,1,41472]{2,1,0:T(1,128)}), f32[8,1,41472]{2,1,0:T(1,128)}) %all-gather.7.cloned.1.call-update) | async-done | bytes 1327120 | tf_op jit(solution)/shard_map/all_gather | solution.py:11
  440.3 2.3 reduce_sum.9
  442.6 0.8 mul.32
  443.4 0.2 mul.35
  443.5 0.9 copy.69
  (33 shorter events, 0.7 us)
Async XLA Ops:
  7.2 392.0 %copy-start = (bf16[27,32,64]{2,1,0:T(8,128)(2,1)S(1)}, bf16[27,32,64]{2,1,0:T(8,128)(2,1)}, u32[]{:S(2)}) copy-start(bf16[27,32,64]{2,1,0:T(8,128)(2,1)} %param.8) | copy-start | bytes 331780
  7.2 24.8 %copy-start.5 = (bf16[27,32,32]{2,1,0:T(8,128)(2,1)S(1)}, bf16[27,32,32]{2,1,0:T(8,128)(2,1)}, u32[]{:S(2)}) copy-start(bf16[27,32,32]{2,1,0:T(8,128)(2,1)} %param.9) | copy-start | bytes 165892
  7.2 30.8 %all-gather.5.cloned.1.call-start = ((), (), s32[]{:S(2)}) async-start(), calls=%async_computation | async-start | bytes 3145728 | tf_op jit(solution)/shard_map/all_gather | solution.py:76
  8.4 11.6 %collective-permute-start.1 = (bf16[16,2,8,512]{3,2,1,0:T(8,128)(2,1)S(1)}, bf16[16,2,8,512]{3,2,1,0:T(8,128)(2,1)S(1)}, u32[]{:S(2)}, u32[]{:S(2)}) collective-permute-start(bf16[16,2,8,512]{3,2,1,0:T(8,128)(2,1)S(1)} %get-tuple-element.21), channel_id=1, source_target_pairs={{2,0},{4,2},{6,4},{8,6},{10,8},{12,10},{14,12},{0,14},{3,1},{5,3},... | collective-permute-start | bytes 786440 | tf_op jit(solution)/shard_map/ppermute | solution.py:25
  14.4 10.5 %collective-permute-start = (bf16[16,2,8,512]{3,2,1,0:T(8,128)(2,1)S(1)}, bf16[16,2,8,512]{3,2,1,0:T(8,128)(2,1)S(1)}, u32[]{:S(2)}, u32[]{:S(2)}) collective-permute-start(bf16[16,2,8,512]{3,2,1,0:T(8,128)(2,1)S(1)} %get-tuple-element.20), channel_id=1, source_target_pairs={{0,2},{2,4},{4,6},{6,8},{8,10},{10,12},{12,14},{14,0},{1,3},{3,5},... | collective-permute-start | bytes 786440 | tf_op jit(solution)/shard_map/ppermute | solution.py:22
  27.0 413.2 %all-gather.7.cloned.1.call-start = ((), (), s32[]{:S(2)}) async-start(), calls=%async_computation.1 | async-start | bytes 1492992 | tf_op jit(solution)/shard_map/all_gather | solution.py:11
  58.3 18.8 %copy-start.7 = (pred[8,65]{0,1:T(8,128)(4,1)S(1)}, pred[8,65]{0,1:T(8,128)(4,1)}, u32[]{:S(2)}) copy-start(pred[8,65]{0,1:T(8,128)(4,1)} %constant.39) | copy-start | bytes 1564
  103.4 7.4 %copy-start.4 = (bf16[16,4,8,512]{3,2,1,0:T(8,128)(2,1)S(1)}, bf16[16,4,8,512]{3,2,1,0:T(8,128)(2,1)}, u32[]{:S(2)}) copy-start(bf16[16,4,8,512]{3,2,1,0:T(8,128)(2,1)} %param.6) | copy-start | bytes 1572868
  112.6 0.8 copy-start.1
  114.1 233.2 %collective-permute-start.2 = (bf16[16,1,8,512]{3,0,2,1:T(8,128)(2,1)}, bf16[16,1,8,512]{3,0,2,1:T(8,128)(2,1)}, u32[]{:S(2)}, u32[]{:S(2)}) collective-permute-start(bf16[16,1,8,512]{3,0,2,1:T(8,128)(2,1)} %slice.46), channel_id=1, source_target_pairs={{14,0},{0,2},{2,4},{4,6},{6,8},{8,10},{10,12},{12,14},{15,1},{1,3}... | collective-permute-start | bytes 393224 | tf_op jit(solution)/shard_map/ppermute | solution.py:33
  174.0 173.3 %copy-start.2 = (bf16[16,4,8,512]{3,0,2,1:T(8,128)(2,1)S(1)}, bf16[16,4,8,512]{3,0,2,1:T(8,128)(2,1)}, u32[]{:S(2)}) copy-start(bf16[16,4,8,512]{3,0,2,1:T(8,128)(2,1)} %copy-done.1) | copy-start | bytes 1572868
  348.9 21.1 %copy-start.3 = (bf16[1,64,2,4,256]{1,0,4,3,2:T(2,128)(2,1)S(1)}, bf16[1,64,2,4,256]{1,0,4,3,2:T(2,128)(2,1)}, u32[]{:S(2)}) copy-start(bf16[1,64,2,4,256]{1,0,4,3,2:T(2,128)(2,1)} %copy.65) | copy-start | bytes 786436
  370.0 27.9 %copy-start.6 = (u32[32]{0:T(128)S(1)}, u32[32]{0:T(128)}, u32[]{:S(2)}) copy-start(u32[32]{0:T(128)} %constant.42) | copy-start | bytes 388
  397.9 9.3 %copy-start.8 = (pred[8,33]{0,1:T(8,128)(4,1)S(1)}, pred[8,33]{0,1:T(8,128)(4,1)}, u32[]{:S(2)}) copy-start(pred[8,33]{0,1:T(8,128)(4,1)} %constant.38) | copy-start | bytes 796
Sparse Core Ops, SparseCore 0:
  27.2 10.7 all-gather.4
  398.0 42.1 all-gather.6
